TPU v7x, 128 devices: a whole 4x4x4 slice. The times are simulated.
128 devices in a mesh: row: 4 (over z_hi, core), circ: 32 (over x, y, z_lo).
Axes of the slice: x: 4, y: 4, z: 4 (z_hi: 2, z_lo: 2; z = z_hi * 2 + z_lo), core: 2. Of those that a mesh axis runs over, the one named last changes fastest.
Arguments:
- flow_state: float32 [5, 64, 32, 4096], P(None, 'row', None, 'circ'), may hold values from -4 to 4
- velocity: float32 [3, 64, 32, 4096], P(None, 'row', None, 'circ'), may hold values from -3 to 3
- offsets: int32 [3, 3], replicated, may hold values from 0 to 4095, as said below
- passage_shift: int32 [4], replicated, may hold values from 0 to 31, as said below
- donor_step: int32 [4, 2, 4096], P('row', None, 'circ'), may hold values from 0 to 127
- donor_weight: float32 [4, 2, 4096], P('row', None, 'circ'), may hold values from 0.05 to 0.95
Outputs:
- updated_state: float32 [5, 64, 32, 4096], P(None, 'row', None, 'circ')
Inputs may be any that keep to these rules, and one draw needn't show every extreme that they name: Rotation offsets in cells; some interface takes the offset 4096 - 1 at some section in every draw, and with two or more interfaces some takes 0. `passage_shift`: passage index placed on device column 0 of each row; some row has 32 - 1 and some row 0 in every draw.
All inputs are finite; a program needn't handle non-finite values.
Results may differ from a plain program's by a relative error of at most 0.0003.
Values sent between devices are 32-bit elements; how exact they have to be, the bound alone decides.
No kernel may reach another device: no remote copies, remote signals or barrier semaphores. Data moves between devices by JAX's collectives and lax.ppermute only.
A program may use at most 128 MiB of HBM per device.

v0:
```python
import jax
import jax.numpy as jnp
from jax import lax
from jax.sharding import PartitionSpec as P

SMAG_COEF = 0.1
TIME_STEP = 0.25


def passed_along(value, axis, steps):
    count = lax.axis_size(axis)
    first, last = (max(0, -steps), min(count, count - steps))
    return lax.ppermute(value, axis, [(source, source + steps) for source in range(first, last)])


def extended(cells, sides, width):
    for axis, dim in sides:
        count = lax.axis_size(axis)
        head = lax.slice_in_dim(cells, 0, width, axis=dim)
        tail = lax.slice_in_dim(cells, cells.shape[dim] - width, cells.shape[dim], axis=dim)
        cells = jnp.concatenate(
            [
                lax.ppermute(tail, axis, [(i, (i + 1) % count) for i in range(count)]),
                cells,
                lax.ppermute(head, axis, [((i + 1) % count, i) for i in range(count)]),
            ],
            axis=dim,
        )
    return cells


def combine(fields, axial_ext, radial_ext, around_ext, velocity):
    d_axial = 0.5 * (axial_ext[:, 2:] - axial_ext[:, :-2])
    d_radial = 0.5 * (radial_ext[:, :, 2:] - radial_ext[:, :, :-2])
    d_around = 0.5 * (around_ext[..., 2:] - around_ext[..., :-2])
    laplace = (
        axial_ext[:, 2:]
        + axial_ext[:, :-2]
        + radial_ext[:, :, 2:]
        + radial_ext[:, :, :-2]
        + around_ext[..., 2:]
        + around_ext[..., :-2]
        - 6.0 * fields
    )
    strain = jnp.sum(d_axial[1:4] ** 2 + d_radial[1:4] ** 2 + d_around[1:4] ** 2, axis=0)
    eddy_visc = SMAG_COEF * jnp.sqrt(strain + 1.0)
    return eddy_visc * laplace - (
        velocity[0] * d_axial + velocity[1] * d_radial + velocity[2] * d_around
    )


def radial_pad(fields):
    return jnp.concatenate([fields[:, :, :1], fields, fields[:, :, -1:]], axis=2)


def axial_pad(fields, lower_ghost, upper_ghost):
    return jnp.concatenate([lower_ghost[:, None], fields, upper_ghost[:, None]], axis=1)


def local(flow_state, velocity, offsets, passage_shift, donor_step, donor_weight):
    row_count = lax.axis_size("row")
    loop_size = lax.axis_size("circ")
    row_id = lax.axis_index("row")
    column = lax.axis_index("circ")
    pitch_cells = flow_state.shape[-1]
    loop_cells = pitch_cells * loop_size
    passage = (column - passage_shift[row_id]) % loop_size
    lower_src = jnp.maximum(row_id - 1, 0)
    upper_src = jnp.minimum(row_id + 1, row_count - 1)
    lower_face = jnp.maximum(row_id - 1, 0)
    upper_face = jnp.minimum(row_id, row_count - 2)
    within = jnp.arange(pitch_cells, dtype=jnp.int32)

    def interface(face_plane, source_row, offset, donor_steps, weights):
        gathered = lax.all_gather(face_plane, "circ", axis=2, tiled=True)
        ordered = jnp.roll(gathered, -passage_shift[source_row] * pitch_cells, axis=2)
        donor_cols = (passage * pitch_cells + within + offset + donor_steps) % loop_cells
        next_cols = (donor_cols + 1) % loop_cells
        return weights * jnp.take(ordered, donor_cols, axis=2) + (1.0 - weights) * jnp.take(
            ordered, next_cols, axis=2
        )

    def evaluate(fields, section_index):
        first_plane = fields[:, 0]
        last_plane = fields[:, -1]
        from_below = passed_along(last_plane, "row", 1)
        from_above = passed_along(first_plane, "row", -1)
        low_offset = offsets[section_index, lower_face]
        high_offset = (loop_cells - offsets[section_index, upper_face]) % loop_cells
        lower_ghost = interface(
            from_below, lower_src, low_offset, donor_step[0, 0], donor_weight[0, 0]
        )
        upper_ghost = interface(
            from_above, upper_src, high_offset, donor_step[0, 1], donor_weight[0, 1]
        )
        lower_ghost = jnp.where(row_id == 0, first_plane, lower_ghost)
        upper_ghost = jnp.where(row_id == row_count - 1, last_plane, upper_ghost)
        around_ext = extended(fields, (("circ", 3),), 1)
        return combine(
            fields,
            axial_pad(fields, lower_ghost, upper_ghost),
            radial_pad(fields),
            around_ext,
            velocity,
        )

    section_one = flow_state + TIME_STEP * evaluate(flow_state, 0)
    section_two = 0.75 * flow_state + 0.25 * (section_one + TIME_STEP * evaluate(section_one, 1))
    return 1.0 / 3.0 * flow_state + 2.0 / 3.0 * (section_two + TIME_STEP * evaluate(section_two, 2))


def solution(mesh):
    placed = (
        P(None, "row", None, "circ"),
        P(None, "row", None, "circ"),
        P(),
        P(),
        P("row", None, "circ"),
        P("row", None, "circ"),
    )
    return jax.shard_map(
        local, mesh=mesh, in_specs=placed, out_specs=P(None, "row", None, "circ"), check_vma=False
    )
```

profile of v0, /device:TPU:0, one launch (start us, length us, event | category | flops | bytes accessed | tf_op | source)
XLA Modules:
  0.0 955.3 jit_solution(16857114506774725180)
XLA Ops:
  11.4 6.9 collective-permute-start.1
  25.1 5.7 collective-permute-start.2
  46.7 101.4 %all-gather.7.cloned.1.call-done = f32[5,32,4096]{2,1,0:T(8,128)} async-done(((f32[5,32,128]{2,1,0:T(8,128)}), f32[5,32,4096]{2,1,0:T(8,128)}) %all-gather.7.cloned.1.call-update) | async-done | bytes 2621456 | tf_op jit(solution)/shard_map/all_gather | solution.py:75
  152.8 9.6 %copy.302 = f32[5,32,4096]{1,0,2:T(8,128)} copy(f32[5,32,4096]{2,1,0:T(8,128)} %fusion.5) | data formatting | bytes 5242880
  162.4 7.2 gather_fusion.1
  171.5 7.4 gather_fusion
  180.6 101.7 %all-gather.9.cloned.1.call-done = f32[5,32,4096]{2,1,0:T(8,128)} async-done(((f32[5,32,128]{2,1,0:T(8,128)}), f32[5,32,4096]{2,1,0:T(8,128)}) %all-gather.9.cloned.1.call-update) | async-done | bytes 2621456 | tf_op jit(solution)/shard_map/all_gather | solution.py:75
  282.4 4.7 fusion.4
  287.1 9.6 %copy.303 = f32[5,32,4096]{1,0,2:T(8,128)} copy(f32[5,32,4096]{2,1,0:T(8,128)} %fusion.4) | data formatting | bytes 5242880
  296.7 7.2 gather_fusion.2
  305.8 7.3 gather_fusion.3
  325.8 5.9 collective-permute-start.5
  346.9 6.3 collective-permute-done.7
  355.7 103.6 %all-gather.11.cloned.1.call-done = f32[5,32,4096]{2,1,0:T(8,128)} async-done(((f32[5,32,128]{2,1,0:T(8,128)}), f32[5,32,4096]{2,1,0:T(8,128)}) %all-gather.11.cloned.1.call-update) | async-done | bytes 2621456 | tf_op jit(solution)/shard_map/all_gather | solution.py:75
  463.9 9.6 %copy.308 = f32[5,32,4096]{1,0,2:T(8,128)} copy(f32[5,32,4096]{2,1,0:T(8,128)} %fusion.3) | data formatting | bytes 5242880
  473.6 7.3 gather_fusion.5
  482.7 7.4 gather_fusion.4
  491.9 102.5 %all-gather.13.cloned.1.call-done = f32[5,32,4096]{2,1,0:T(8,128)} async-done(((f32[5,32,128]{2,1,0:T(8,128)}), f32[5,32,4096]{2,1,0:T(8,128)}) %all-gather.13.cloned.1.call-update) | async-done | bytes 2621456 | tf_op jit(solution)/shard_map/all_gather | solution.py:75
  594.4 4.7 fusion.2
  599.1 9.6 %copy.309 = f32[5,32,4096]{1,0,2:T(8,128)} copy(f32[5,32,4096]{2,1,0:T(8,128)} %fusion.2) | data formatting | bytes 5242880
  608.8 7.2 gather_fusion.6
  617.8 7.2 gather_fusion.7
  638.4 6.5 collective-permute-start.9
  659.9 6.2 collective-permute-done.11
  668.5 104.5 %all-gather.15.cloned.1.call-done = f32[5,32,4096]{2,1,0:T(8,128)} async-done(((f32[5,32,128]{2,1,0:T(8,128)}), f32[5,32,4096]{2,1,0:T(8,128)}) %all-gather.15.cloned.1.call-update) | async-done | bytes 2621456 | tf_op jit(solution)/shard_map/all_gather | solution.py:75
  777.7 9.6 %copy.312 = f32[5,32,4096]{1,0,2:T(8,128)} copy(f32[5,32,4096]{2,1,0:T(8,128)} %fusion.1) | data formatting | bytes 5242880
  787.3 7.4 gather_fusion.9
  796.5 7.4 gather_fusion.8
  805.7 101.5 %all-gather.17.cloned.1.call-done = f32[5,32,4096]{2,1,0:T(8,128)} async-done(((f32[5,32,128]{2,1,0:T(8,128)}), f32[5,32,4096]{2,1,0:T(8,128)}) %all-gather.17.cloned.1.call-update) | async-done | bytes 2621456 | tf_op jit(solution)/shard_map/all_gather | solution.py:75
  911.9 9.6 %copy.313 = f32[5,32,4096]{1,0,2:T(8,128)} copy(f32[5,32,4096]{2,1,0:T(8,128)} %fusion) | data formatting | bytes 5242880
  921.5 7.2 gather_fusion.10
  930.6 7.2 gather_fusion.11
  (172 shorter events, 129.9 us)
Async XLA Ops:
  6.5 141.6 %all-gather.7.cloned.1.call-start = ((), (), s32[]{:S(2)}) async-start(), calls=%async_computation | async-start | bytes 2703360 | tf_op jit(solution)/shard_map/all_gather | solution.py:75
  7.5 3.2 collective-permute-start
  11.3 271.0 %all-gather.9.cloned.1.call-start = ((), (), s32[]{:S(2)}) async-start(), calls=%async_computation.1 | async-start | bytes 2703360 | tf_op jit(solution)/shard_map/all_gather | solution.py:75
  11.4 7.8 collective-permute-start.1
  19.8 439.5 %all-gather.11.cloned.1.call-start = ((), (), s32[]{:S(2)}) async-start(), calls=%async_computation.2 | async-start | bytes 2703360 | tf_op jit(solution)/shard_map/all_gather | solution.py:75
  25.1 17.9 %collective-permute-start.2 = (f32[5,16,32,1]{2,1,3,0:T(8,128)S(1)}, f32[5,16,32,1]{2,1,3,0:T(8,128)}, u32[]{:S(2)}, u32[]{:S(2)}) collective-permute-start(f32[5,16,32,1]{2,1,3,0:T(8,128)S(1)} %copy.304), channel_id=1, source_target_pairs={{1,0},{2,1},{3,2},{4,3},{5,4},{6,5},{7,6},{8,7},{9,8},{10,9},{11,1... | collective-permute-start | bytes 30728 | tf_op jit(solution)/shard_map/ppermute | solution.py:25
  31.9 12.4 %collective-permute-start.3 = (f32[5,16,32,1]{2,1,3,0:T(8,128)}, f32[5,16,32,1]{2,1,3,0:T(8,128)}, u32[]{:S(2)}, u32[]{:S(2)}) collective-permute-start(f32[5,16,32,1]{2,1,3,0:T(8,128)} %copy.305), channel_id=1, source_target_pairs={{0,1},{1,2},{2,3},{3,4},{4,5},{5,6},{6,7},{7,8},{8,9},{9,10},{10,1... | collective-permute-start | bytes 30728 | tf_op jit(solution)/shard_map/ppermute | solution.py:23
  44.3 271.7 %copy-start.3 = (f32[5,16,32,1]{3,2,1,0:T(8,128)}, f32[5,16,32,1]{3,2,1,0:T(8,128)S(1)}, u32[]{:S(2)}) copy-start(f32[5,16,32,1]{3,2,1,0:T(8,128)S(1)} %copy.269) | copy-start | bytes 30724
  296.7 18.2 %copy-start.14 = (pred[128]{0:T(512)(128)(4,1)S(1)}, pred[128]{0:T(512)(128)(4,1)}, u32[]{:S(2)}) copy-start(pred[128]{0:T(512)(128)(4,1)} %get-tuple-element.25) | copy-start | bytes 388
  296.7 18.2 %copy-start.15 = (pred[128]{0:T(512)(128)(4,1)S(1)}, pred[128]{0:T(512)(128)(4,1)}, u32[]{:S(2)}) copy-start(pred[128]{0:T(512)(128)(4,1)} %get-tuple-element.94) | copy-start | bytes 388
  296.7 18.2 %copy-start.24 = (pred[128]{0:T(512)(128)(4,1)S(1)}, pred[128]{0:T(512)(128)(4,1)}, u32[]{:S(2)}) copy-start(pred[128]{0:T(512)(128)(4,1)} %get-tuple-element.79) | copy-start | bytes 388
  296.7 18.2 %copy-start.25 = (pred[128]{0:T(512)(128)(4,1)S(1)}, pred[128]{0:T(512)(128)(4,1)}, u32[]{:S(2)}) copy-start(pred[128]{0:T(512)(128)(4,1)} %get-tuple-element.81) | copy-start | bytes 388
  322.4 305.6 %copy-start.1 = (f32[5,16,32,128]{3,2,1,0:T(8,128)}, f32[5,16,32,128]{3,2,1,0:T(8,128)S(1)}, u32[]{:S(2)}) copy-start(f32[5,16,32,128]{3,2,1,0:T(8,128)S(1)} %multiply_add_fusion.2) | copy-start | bytes 3932164
  322.4 3.3 collective-permute-start.4
  325.7 268.7 %all-gather.13.cloned.1.call-start = ((), (), s32[]{:S(2)}) async-start(), calls=%async_computation.3 | async-start | bytes 2703360 | tf_op jit(solution)/shard_map/all_gather | solution.py:75
  325.8 6.3 collective-permute-start.5
  332.2 440.9 %all-gather.15.cloned.1.call-start = ((), (), s32[]{:S(2)}) async-start(), calls=%async_computation.4 | async-start | bytes 2703360 | tf_op jit(solution)/shard_map/all_gather | solution.py:75
  338.1 6.5 collective-permute-start.6
  344.5 8.7 collective-permute-start.7
  608.8 18.1 %copy-start.18 = (pred[128]{0:T(512)(128)(4,1)S(1)}, pred[128]{0:T(512)(128)(4,1)}, u32[]{:S(2)}) copy-start(pred[128]{0:T(512)(128)(4,1)} %get-tuple-element.17) | copy-start | bytes 388
  608.8 18.1 %copy-start.19 = (pred[128]{0:T(512)(128)(4,1)S(1)}, pred[128]{0:T(512)(128)(4,1)}, u32[]{:S(2)}) copy-start(pred[128]{0:T(512)(128)(4,1)} %get-tuple-element.92) | copy-start | bytes 388
  608.8 18.1 %copy-start.22 = (pred[128]{0:T(512)(128)(4,1)S(1)}, pred[128]{0:T(512)(128)(4,1)}, u32[]{:S(2)}) copy-start(pred[128]{0:T(512)(128)(4,1)} %get-tuple-element.75) | copy-start | bytes 388
  608.8 18.1 %copy-start.23 = (pred[128]{0:T(512)(128)(4,1)S(1)}, pred[128]{0:T(512)(128)(4,1)}, u32[]{:S(2)}) copy-start(pred[128]{0:T(512)(128)(4,1)} %get-tuple-element.77) | copy-start | bytes 388
  635.0 3.3 collective-permute-start.8
  638.3 268.8 %all-gather.17.cloned.1.call-start = ((), (), s32[]{:S(2)}) async-start(), calls=%async_computation.5 | async-start | bytes 2703360 | tf_op jit(solution)/shard_map/all_gather | solution.py:75
  638.4 6.9 collective-permute-start.9
  651.0 6.6 collective-permute-start.10
  657.5 8.7 collective-permute-start.11
  921.5 18.1 %copy-start.16 = (pred[128]{0:T(512)(128)(4,1)S(1)}, pred[128]{0:T(512)(128)(4,1)}, u32[]{:S(2)}) copy-start(pred[128]{0:T(512)(128)(4,1)} %get-tuple-element.9) | copy-start | bytes 388
  921.5 18.1 %copy-start.17 = (pred[128]{0:T(512)(128)(4,1)S(1)}, pred[128]{0:T(512)(128)(4,1)}, u32[]{:S(2)}) copy-start(pred[128]{0:T(512)(128)(4,1)} %get-tuple-element.90) | copy-start | bytes 388
  921.5 18.1 %copy-start.20 = (pred[128]{0:T(512)(128)(4,1)S(1)}, pred[128]{0:T(512)(128)(4,1)}, u32[]{:S(2)}) copy-start(pred[128]{0:T(512)(128)(4,1)} %get-tuple-element.6) | copy-start | bytes 388
  921.5 18.1 %copy-start.21 = (pred[128]{0:T(512)(128)(4,1)S(1)}, pred[128]{0:T(512)(128)(4,1)}, u32[]{:S(2)}) copy-start(pred[128]{0:T(512)(128)(4,1)} %get-tuple-element.73) | copy-start | bytes 388
  (18 other events, 128.0 us)
Sparse Core Ops, SparseCore 0:
  11.4 136.6 all-gather.6
  149.7 132.6 all-gather.8
  325.9 133.3 all-gather.10
  460.7 133.6 all-gather.12
  638.4 134.5 all-gather.14
  774.4 132.6 all-gather.16
where the time goes:
time: 958 us; the launch traced here: 955 us
  waiting for transfers between devices  635 us (66%)
  local copies, waits for them, and re-layouts  207 us (22%)
  other arithmetic  57.5 us (6%)
  starting transfers between devices  37.3 us (4%)
  between operations  18 us (2%)
    all_gather x6, waiting for transfers between devices, interface(): gathered = lax.all_gather(face_plane, 'circ', axis=2, tiled=True)  615 us
    unnamed x72, local copies, waits for them, and re-layouts  66.2 us
    gather x12, local copies, waits for them, and re-layouts, interface(): jnp.take(ordered, donor_cols, axis=2)  54.6 us
    gather x12, local copies, waits for them, and re-layouts, interface(): jnp.take(ordered, next_cols, axis=2)  54.6 us
    concatenate x6, other arithmetic, interface(): jnp.roll(gathered, -passage_shift[source_row] * pitch_cells, axis=2)  28.1 us
    ppermute x6, starting transfers between devices, passed_along(): lax.ppermute(value, axis, [(source, source + steps) for source in range(f...  23.2 us
  transfers between devices with their start and end apart: 18, of which 14 were waited for; matrix products, arithmetic and copies ran while one was open for 15% of the time, Pallas kernels for 0%

commit v1 on v0

--- a/solution.py
+++ b/solution.py
@@ -72,7 +72,9 @@
     within = jnp.arange(pitch_cells, dtype=jnp.int32)
 
     def interface(face_plane, source_row, offset, donor_steps, weights):
-        gathered = lax.all_gather(face_plane, "circ", axis=2, tiled=True)
+        gathered = jnp.concatenate(
+            lax.all_to_all(jnp.stack([face_plane] * lax.axis_size("circ")), "circ", 0, 0), axis=2
+        )
         ordered = jnp.roll(gathered, -passage_shift[source_row] * pitch_cells, axis=2)
         donor_cols = (passage * pitch_cells + within + offset + donor_steps) % loop_cells
         next_cols = (donor_cols + 1) % loop_cells

time: 958 us -> 481 us (0.50)
  waiting for transfers between devices: 635 us -> 108 us
  starting transfers between devices: 37.3 us -> 84.7 us
  local copies, waits for them, and re-layouts: 207 us -> 229 us
  between operations: 18 us -> 4.67 us
  other arithmetic: 57.5 us -> 45.8 us
    all_gather x6 -> x0, waiting for transfers between devices: 615 us -> none  [interface(): gathered = lax.all_gather(face_plane, 'circ', axis=2, tiled=True)]
    all_to_all x0 -> x6, waiting for transfers between devices: none -> 60.6 us  [interface(): lax.all_to_all(jnp.stack([face_plane] * lax.axis_size('circ')), 'circ', 0...]
    all_to_all x0 -> x6, starting transfers between devices: none -> 43.2 us  [interface(): lax.all_to_all(jnp.stack([face_plane] * lax.axis_size('circ')), 'circ', 0...]
    ppermute x3, waiting for transfers between devices: 0.01 us -> 19 us  [extended(): lax.ppermute(head, axis, [((i + 1) % count, i) for i in range(count)])]
    another operation x0 -> x6, local copies, waits for them, and re-layouts: none -> 12.7 us  [interface(): jnp.stack([face_plane] * lax.axis_size('circ'))]
    reshape x0 -> x6, local copies, waits for them, and re-layouts: none -> 12.1 us  [interface(): jnp.concatenate(lax.all_to_all(jnp.stack([face_plane] * lax.axis_size('ci...]
    concatenate x6, other arithmetic: 28.1 us -> 17.7 us  [interface(): jnp.roll(gathered, -passage_shift[source_row] * pitch_cells, axis=2)]
    unnamed x72 -> x70, local copies, waits for them, and re-layouts: 66.2 us -> 65.1 us
  transfers between devices with their start and end apart: 18 -> 18, of which waited for: 14 -> 12; matrix products, arithmetic and copies ran while one was open for 15% -> 30% of each run, Pallas kernels for 0% -> 0%
where the time goes in v1:
time: 481 us; the launch traced here: 472 us
  local copies, waits for them, and re-layouts  229 us (48%)
  waiting for transfers between devices  108 us (22%)
  starting transfers between devices  84.7 us (18%)
  other arithmetic  45.8 us (10%)
    unnamed x70, local copies, waits for them, and re-layouts  65.1 us
    all_to_all x6, waiting for transfers between devices, interface(): lax.all_to_all(jnp.stack([face_plane] * lax.axis_size('circ')), 'circ', 0...  60.6 us
    gather x12, local copies, waits for them, and re-layouts, interface(): jnp.take(ordered, donor_cols, axis=2)  54.5 us
    gather x12, local copies, waits for them, and re-layouts, interface(): jnp.take(ordered, next_cols, axis=2)  54.5 us
    all_to_all x6, starting transfers between devices, interface(): lax.all_to_all(jnp.stack([face_plane] * lax.axis_size('circ')), 'circ', 0...  43.2 us
    ppermute x6, starting transfers between devices, passed_along(): lax.ppermute(value, axis, [(source, source + steps) for source in range(f...  23.1 us
    ppermute x3, waiting for transfers between devices, extended(): lax.ppermute(tail, axis, [(i, (i + 1) % count) for i in range(count)])  20.3 us
    ppermute x3, waiting for transfers between devices, extended(): lax.ppermute(head, axis, [((i + 1) % count, i) for i in range(count)])  19 us
  transfers between devices with their start and end apart: 18, of which 12 were waited for; matrix products, arithmetic and copies ran while one was open for 30% of the time, Pallas kernels for 0%

profile of v1, /device:TPU:0, one launch (start us, length us, event | category | flops | bytes accessed | tf_op | source)
XLA Modules:
  0.0 471.7 jit_solution(6113354366230017445)
XLA Ops:
  5.9 9.0 %all-to-all-start = ((f32[32,5,32,128]{3,2,1,0:T(8,128)}), f32[32,5,32,128]{3,2,1,0:T(8,128)}, u32[]{:S(2)}, u32[]{:S(2)}) async-start(f32[32,5,32,128]{3,2,1,0:T(8,128)} %stack.12), calls=%async_computation | async-start | bytes 5242880 | tf_op jit(solution)/shard_map/all_to_all | solution.py:76
  37.9 11.6 %all-to-all-done = f32[32,5,32,128]{3,2,1,0:T(8,128)} async-done(((f32[32,5,32,128]{3,2,1,0:T(8,128)}), f32[32,5,32,128]{3,2,1,0:T(8,128)}, u32[]{:S(2)}, u32[]{:S(2)}) %all-to-all-start) | async-done | bytes 2621472 | tf_op jit(solution)/shard_map/all_to_all | solution.py:76
  68.7 9.7 %copy.349 = f32[5,32,4096]{1,0,2:T(8,128)} copy(f32[5,32,4096]{2,1,0:T(8,128)} %fusion.5) | data formatting | bytes 5242880
  78.4 7.2 %gather_fusion.1 = f32[128,5,32]{2,1,0:T(8,128)} fusion(f32[5,32,4096]{1,0,2:T(8,128)} %copy.349, s32[1024]{0:T(1024)S(1)} %pad_clamp_fusion.10), kind=kCustom, calls=%fused_computation.1.clone | custom fusion | bytes 164352 | tf_op jit(solution)/shard_map/jit(_take)/gather | solution.py:81
  87.4 7.3 %gather_fusion = f32[128,5,32]{2,1,0:T(8,128)} fusion(f32[5,32,4096]{1,0,2:T(8,128)} %copy.349, s32[1024]{0:T(1024)} %pad_clamp_fusion.11), kind=kCustom, calls=%fused_computation.clone | custom fusion | bytes 164352 | tf_op jit(solution)/shard_map/jit(_take)/gather | solution.py:81
  101.5 9.7 %copy.350 = f32[5,32,4096]{1,0,2:T(8,128)} copy(f32[5,32,4096]{2,1,0:T(8,128)} %fusion.4) | data formatting | bytes 5242880
  111.2 7.2 %gather_fusion.2 = f32[128,5,32]{2,1,0:T(8,128)} fusion(f32[5,32,4096]{1,0,2:T(8,128)} %copy.350, s32[1024]{0:T(1024)S(1)} %pad_clamp_fusion.9), kind=kCustom, calls=%fused_computation.2.clone | custom fusion | bytes 164352 | tf_op jit(solution)/shard_map/jit(_take)/gather | solution.py:81
  120.2 7.3 %gather_fusion.3 = f32[128,5,32]{2,1,0:T(8,128)} fusion(f32[5,32,4096]{1,0,2:T(8,128)} %copy.350, s32[1024]{0:T(1024)} %pad_clamp_fusion.8), kind=kCustom, calls=%fused_computation.3.clone | custom fusion | bytes 164352 | tf_op jit(solution)/shard_map/jit(_take)/gather | solution.py:81
  143.0 8.4 %all-to-all-start.2 = ((f32[32,5,32,128]{3,2,1,0:T(8,128)}), f32[32,5,32,128]{3,2,1,0:T(8,128)}, u32[]{:S(2)}, u32[]{:S(2)}) async-start(f32[32,5,32,128]{3,2,1,0:T(8,128)} %stack.14), calls=%async_computation.2 | async-start | bytes 5242880 | tf_op jit(solution)/shard_map/all_to_all | solution.py:76
  152.0 6.8 %collective-permute-start.5 = (f32[5,32,128]{2,1,0:T(8,128)S(1)}, f32[5,32,128]{2,1,0:T(8,128)}, u32[]{:S(2)}, u32[]{:S(2)}) collective-permute-start(f32[5,32,128]{2,1,0:T(8,128)S(1)} %get-tuple-element.49), channel_id=1, source_target_pairs={{0,32},{32,64},{64,96},{1,33},{33,65},{65,97},{2,34},{34,66},{66,9... | collective-permute-start | bytes 245768 | tf_op jit(solution)/shard_map/ppermute | solution.py:13
  159.2 24.5 %all-to-all-done.2 = f32[32,5,32,128]{3,2,1,0:T(8,128)} async-done(((f32[32,5,32,128]{3,2,1,0:T(8,128)}), f32[32,5,32,128]{3,2,1,0:T(8,128)}, u32[]{:S(2)}, u32[]{:S(2)}) %all-to-all-start.2) | async-done | bytes 2621472 | tf_op jit(solution)/shard_map/all_to_all | solution.py:76
  197.5 6.1 %collective-permute-start.6 = (f32[5,16,32,1]{2,1,3,0:T(8,128)S(1)}, f32[5,16,32,1]{2,1,3,0:T(8,128)}, u32[]{:S(2)}, u32[]{:S(2)}) collective-permute-start(f32[5,16,32,1]{2,1,3,0:T(8,128)S(1)} %copy.327), channel_id=1, source_target_pairs={{1,0},{2,1},{3,2},{4,3},{5,4},{6,5},{7,6},{8,7},{9,8},{10,9},{11,1... | collective-permute-start | bytes 30728 | tf_op jit(solution)/shard_map/ppermute | solution.py:25
  206.2 9.5 %collective-permute-done.6 = f32[5,16,32,1]{2,1,3,0:T(8,128)} collective-permute-done((f32[5,16,32,1]{2,1,3,0:T(8,128)S(1)}, f32[5,16,32,1]{2,1,3,0:T(8,128)}, u32[]{:S(2)}, u32[]{:S(2)}) %collective-permute-start.6) | collective-permute-done | bytes 10272 | tf_op jit(solution)/shard_map/ppermute | solution.py:25
  218.2 10.2 %collective-permute-done.7 = f32[5,16,32,1]{2,1,3,0:T(8,128)} collective-permute-done((f32[5,16,32,1]{2,1,3,0:T(8,128)}, f32[5,16,32,1]{2,1,3,0:T(8,128)}, u32[]{:S(2)}, u32[]{:S(2)}) %collective-permute-start.7) | collective-permute-done | bytes 10272 | tf_op jit(solution)/shard_map/ppermute | solution.py:23
  235.7 9.7 %copy.355 = f32[5,32,4096]{1,0,2:T(8,128)} copy(f32[5,32,4096]{2,1,0:T(8,128)} %fusion.3) | data formatting | bytes 5242880
  245.4 7.3 %gather_fusion.5 = f32[128,5,32]{2,1,0:T(8,128)} fusion(f32[5,32,4096]{1,0,2:T(8,128)} %copy.355, s32[1024]{0:T(1024)} %pad_clamp_fusion.6), kind=kCustom, calls=%fused_computation.5.clone | custom fusion | bytes 164352 | tf_op jit(solution)/shard_map/jit(_take)/gather | solution.py:81
  254.5 7.3 %gather_fusion.4 = f32[128,5,32]{2,1,0:T(8,128)} fusion(f32[5,32,4096]{1,0,2:T(8,128)} %copy.355, s32[1024]{0:T(1024)} %pad_clamp_fusion.7), kind=kCustom, calls=%fused_computation.4.clone | custom fusion | bytes 164352 | tf_op jit(solution)/shard_map/jit(_take)/gather | solution.py:81
  268.6 9.7 %copy.356 = f32[5,32,4096]{1,0,2:T(8,128)} copy(f32[5,32,4096]{2,1,0:T(8,128)} %fusion.2) | data formatting | bytes 5242880
  278.3 7.2 %gather_fusion.6 = f32[128,5,32]{2,1,0:T(8,128)} fusion(f32[5,32,4096]{1,0,2:T(8,128)} %copy.356, s32[1024]{0:T(1024)S(1)} %pad_clamp_fusion.5), kind=kCustom, calls=%fused_computation.6.clone | custom fusion | bytes 164352 | tf_op jit(solution)/shard_map/jit(_take)/gather | solution.py:81
  287.4 7.2 %gather_fusion.7 = f32[128,5,32]{2,1,0:T(8,128)} fusion(f32[5,32,4096]{1,0,2:T(8,128)} %copy.356, s32[1024]{0:T(1024)S(1)} %pad_clamp_fusion.4), kind=kCustom, calls=%fused_computation.7.clone | custom fusion | bytes 164352 | tf_op jit(solution)/shard_map/jit(_take)/gather | solution.py:81
  309.7 8.0 %all-to-all-start.4 = ((f32[32,5,32,128]{3,2,1,0:T(8,128)}), f32[32,5,32,128]{3,2,1,0:T(8,128)}, u32[]{:S(2)}, u32[]{:S(2)}) async-start(f32[32,5,32,128]{3,2,1,0:T(8,128)} %stack.16), calls=%async_computation.4 | async-start | bytes 5242880 | tf_op jit(solution)/shard_map/all_to_all | solution.py:76
  318.2 6.8 %collective-permute-start.9 = (f32[5,32,128]{2,1,0:T(8,128)S(1)}, f32[5,32,128]{2,1,0:T(8,128)}, u32[]{:S(2)}, u32[]{:S(2)}) collective-permute-start(f32[5,32,128]{2,1,0:T(8,128)S(1)} %get-tuple-element.38), channel_id=1, source_target_pairs={{0,32},{32,64},{64,96},{1,33},{33,65},{65,97},{2,34},{34,66},{66,9... | collective-permute-start | bytes 245768 | tf_op jit(solution)/shard_map/ppermute | solution.py:13
  325.5 24.6 %all-to-all-done.4 = f32[32,5,32,128]{3,2,1,0:T(8,128)} async-done(((f32[32,5,32,128]{3,2,1,0:T(8,128)}), f32[32,5,32,128]{3,2,1,0:T(8,128)}, u32[]{:S(2)}, u32[]{:S(2)}) %all-to-all-start.4) | async-done | bytes 2621472 | tf_op jit(solution)/shard_map/all_to_all | solution.py:76
  363.7 6.1 %collective-permute-start.10 = (f32[5,16,32,1]{2,1,3,0:T(8,128)S(1)}, f32[5,16,32,1]{2,1,3,0:T(8,128)}, u32[]{:S(2)}, u32[]{:S(2)}) collective-permute-start(f32[5,16,32,1]{2,1,3,0:T(8,128)S(1)} %copy.343), channel_id=1, source_target_pairs={{1,0},{2,1},{3,2},{4,3},{5,4},{6,5},{7,6},{8,7},{9,8},{10,9},{11,1... | collective-permute-start | bytes 30728 | tf_op jit(solution)/shard_map/ppermute | solution.py:25
  372.5 9.5 %collective-permute-done.10 = f32[5,16,32,1]{2,1,3,0:T(8,128)} collective-permute-done((f32[5,16,32,1]{2,1,3,0:T(8,128)S(1)}, f32[5,16,32,1]{2,1,3,0:T(8,128)}, u32[]{:S(2)}, u32[]{:S(2)}) %collective-permute-start.10) | collective-permute-done | bytes 10272 | tf_op jit(solution)/shard_map/ppermute | solution.py:25
  384.4 10.2 %collective-permute-done.11 = f32[5,16,32,1]{2,1,3,0:T(8,128)} collective-permute-done((f32[5,16,32,1]{2,1,3,0:T(8,128)}, f32[5,16,32,1]{2,1,3,0:T(8,128)}, u32[]{:S(2)}, u32[]{:S(2)}) %collective-permute-start.11) | collective-permute-done | bytes 10272 | tf_op jit(solution)/shard_map/ppermute | solution.py:23
  402.0 9.7 %copy.359 = f32[5,32,4096]{1,0,2:T(8,128)} copy(f32[5,32,4096]{2,1,0:T(8,128)} %fusion.1) | data formatting | bytes 5242880
  411.7 7.3 %gather_fusion.9 = f32[128,5,32]{2,1,0:T(8,128)} fusion(f32[5,32,4096]{1,0,2:T(8,128)} %copy.359, s32[1024]{0:T(1024)} %pad_clamp_fusion.2), kind=kCustom, calls=%fused_computation.9.clone | custom fusion | bytes 164352 | tf_op jit(solution)/shard_map/jit(_take)/gather | solution.py:81
  420.8 7.3 %gather_fusion.8 = f32[128,5,32]{2,1,0:T(8,128)} fusion(f32[5,32,4096]{1,0,2:T(8,128)} %copy.359, s32[1024]{0:T(1024)} %pad_clamp_fusion.3), kind=kCustom, calls=%fused_computation.8.clone | custom fusion | bytes 164352 | tf_op jit(solution)/shard_map/jit(_take)/gather | solution.py:81
  434.9 9.7 %copy.360 = f32[5,32,4096]{1,0,2:T(8,128)} copy(f32[5,32,4096]{2,1,0:T(8,128)} %fusion) | data formatting | bytes 5242880
  444.6 7.2 %gather_fusion.10 = f32[128,5,32]{2,1,0:T(8,128)} fusion(f32[5,32,4096]{1,0,2:T(8,128)} %copy.360, s32[1024]{0:T(1024)S(1)} %pad_clamp_fusion.1), kind=kCustom, calls=%fused_computation.10.clone | custom fusion | bytes 164352 | tf_op jit(solution)/shard_map/jit(_take)/gather | solution.py:81
  453.6 7.2 %gather_fusion.11 = f32[128,5,32]{2,1,0:T(8,128)} fusion(f32[5,32,4096]{1,0,2:T(8,128)} %copy.360, s32[1024]{0:T(1024)S(1)} %pad_clamp_fusion), kind=kCustom, calls=%fused_computation.11.clone | custom fusion | bytes 164352 | tf_op jit(solution)/shard_map/jit(_take)/gather | solution.py:81
  (173 shorter events, 170.3 us)
Async XLA Ops:
  0.9 3.2 collective-permute-start
  5.9 43.5 %all-to-all-start = ((f32[32,5,32,128]{3,2,1,0:T(8,128)}), f32[32,5,32,128]{3,2,1,0:T(8,128)}, u32[]{:S(2)}, u32[]{:S(2)}) async-start(f32[32,5,32,128]{3,2,1,0:T(8,128)} %stack.12), calls=%async_computation | async-start | bytes 5242880 | tf_op jit(solution)/shard_map/all_to_all | solution.py:76
  15.0 22.9 %collective-permute-start.1 = (f32[5,32,128]{2,1,0:T(8,128)S(1)}, f32[5,32,128]{2,1,0:T(8,128)S(1)}, u32[]{:S(2)}, u32[]{:S(2)}) collective-permute-start(f32[5,32,128]{2,1,0:T(8,128)S(1)} %get-tuple-element.60), channel_id=1, source_target_pairs={{0,32},{32,64},{64,96},{1,33},{33,65},{65,97},{2,34},{34,66},{66,9... | collective-permute-start | bytes 245768 | tf_op jit(solution)/shard_map/ppermute | solution.py:13
  24.0 35.9 %collective-permute-start.2 = (f32[5,16,32,1]{2,1,3,0:T(8,128)S(1)}, f32[5,16,32,1]{2,1,3,0:T(8,128)}, u32[]{:S(2)}, u32[]{:S(2)}) collective-permute-start(f32[5,16,32,1]{2,1,3,0:T(8,128)S(1)} %copy.351), channel_id=1, source_target_pairs={{1,0},{2,1},{3,2},{4,3},{5,4},{6,5},{7,6},{8,7},{9,8},{10,9},{11,1... | collective-permute-start | bytes 30728 | tf_op jit(solution)/shard_map/ppermute | solution.py:25
  30.9 30.3 %collective-permute-start.3 = (f32[5,16,32,1]{2,1,3,0:T(8,128)}, f32[5,16,32,1]{2,1,3,0:T(8,128)}, u32[]{:S(2)}, u32[]{:S(2)}) collective-permute-start(f32[5,16,32,1]{2,1,3,0:T(8,128)} %copy.352), channel_id=1, source_target_pairs={{0,1},{1,2},{2,3},{3,4},{4,5},{5,6},{6,7},{7,8},{8,9},{9,10},{10,1... | collective-permute-start | bytes 30728 | tf_op jit(solution)/shard_map/ppermute | solution.py:23
  51.3 45.3 %all-to-all-start.1 = ((f32[32,5,32,128]{3,2,1,0:T(8,128)}), f32[32,5,32,128]{3,2,1,0:T(8,128)}, u32[]{:S(2)}, u32[]{:S(2)}) async-start(f32[32,5,32,128]{3,2,1,0:T(8,128)} %stack.13), calls=%async_computation.1 | async-start | bytes 5242880 | tf_op jit(solution)/shard_map/all_to_all | solution.py:76
  61.2 69.2 %copy-start.3 = (f32[5,16,32,1]{3,2,1,0:T(8,128)}, f32[5,16,32,1]{3,2,1,0:T(8,128)S(1)}, u32[]{:S(2)}) copy-start(f32[5,16,32,1]{3,2,1,0:T(8,128)S(1)} %copy.312) | copy-start | bytes 30724
  111.2 18.2 %copy-start.17 = (pred[128]{0:T(512)(128)(4,1)S(1)}, pred[128]{0:T(512)(128)(4,1)}, u32[]{:S(2)}) copy-start(pred[128]{0:T(512)(128)(4,1)} %get-tuple-element.25) | copy-start | bytes 388
  111.2 18.2 %copy-start.18 = (pred[128]{0:T(512)(128)(4,1)S(1)}, pred[128]{0:T(512)(128)(4,1)}, u32[]{:S(2)}) copy-start(pred[128]{0:T(512)(128)(4,1)} %get-tuple-element.94) | copy-start | bytes 388
  111.2 18.2 %copy-start.27 = (pred[128]{0:T(512)(128)(4,1)S(1)}, pred[128]{0:T(512)(128)(4,1)}, u32[]{:S(2)}) copy-start(pred[128]{0:T(512)(128)(4,1)} %get-tuple-element.79) | copy-start | bytes 388
  111.2 18.2 %copy-start.28 = (pred[128]{0:T(512)(128)(4,1)S(1)}, pred[128]{0:T(512)(128)(4,1)}, u32[]{:S(2)}) copy-start(pred[128]{0:T(512)(128)(4,1)} %get-tuple-element.81) | copy-start | bytes 388
  136.8 160.7 %copy-start.1 = (f32[5,16,32,128]{3,2,1,0:T(8,128)}, f32[5,16,32,128]{3,2,1,0:T(8,128)S(1)}, u32[]{:S(2)}) copy-start(f32[5,16,32,128]{3,2,1,0:T(8,128)S(1)} %multiply_add_fusion.2) | copy-start | bytes 3932164
  136.9 4.3 collective-permute-start.4
  143.0 40.7 %all-to-all-start.2 = ((f32[32,5,32,128]{3,2,1,0:T(8,128)}), f32[32,5,32,128]{3,2,1,0:T(8,128)}, u32[]{:S(2)}, u32[]{:S(2)}) async-start(f32[32,5,32,128]{3,2,1,0:T(8,128)} %stack.14), calls=%async_computation.2 | async-start | bytes 5242880 | tf_op jit(solution)/shard_map/all_to_all | solution.py:76
  152.0 7.2 %collective-permute-start.5 = (f32[5,32,128]{2,1,0:T(8,128)S(1)}, f32[5,32,128]{2,1,0:T(8,128)}, u32[]{:S(2)}, u32[]{:S(2)}) collective-permute-start(f32[5,32,128]{2,1,0:T(8,128)S(1)} %get-tuple-element.49), channel_id=1, source_target_pairs={{0,32},{32,64},{64,96},{1,33},{33,65},{65,97},{2,34},{34,66},{66,9... | collective-permute-start | bytes 245768 | tf_op jit(solution)/shard_map/ppermute | solution.py:13
  186.4 77.3 %all-to-all-start.3 = ((f32[32,5,32,128]{3,2,1,0:T(8,128)}), f32[32,5,32,128]{3,2,1,0:T(8,128)}, u32[]{:S(2)}, u32[]{:S(2)}) async-start(f32[32,5,32,128]{3,2,1,0:T(8,128)} %stack.15), calls=%async_computation.3 | async-start | bytes 5242880 | tf_op jit(solution)/shard_map/all_to_all | solution.py:76
  197.5 18.3 %collective-permute-start.6 = (f32[5,16,32,1]{2,1,3,0:T(8,128)S(1)}, f32[5,16,32,1]{2,1,3,0:T(8,128)}, u32[]{:S(2)}, u32[]{:S(2)}) collective-permute-start(f32[5,16,32,1]{2,1,3,0:T(8,128)S(1)} %copy.327), channel_id=1, source_target_pairs={{1,0},{2,1},{3,2},{4,3},{5,4},{6,5},{7,6},{8,7},{9,8},{10,9},{11,1... | collective-permute-start | bytes 30728 | tf_op jit(solution)/shard_map/ppermute | solution.py:25
  206.0 22.3 %collective-permute-start.7 = (f32[5,16,32,1]{2,1,3,0:T(8,128)}, f32[5,16,32,1]{2,1,3,0:T(8,128)}, u32[]{:S(2)}, u32[]{:S(2)}) collective-permute-start(f32[5,16,32,1]{2,1,3,0:T(8,128)} %copy.329), channel_id=1, source_target_pairs={{0,1},{1,2},{2,3},{3,4},{4,5},{5,6},{6,7},{7,8},{8,9},{9,10},{10,1... | collective-permute-start | bytes 30728 | tf_op jit(solution)/shard_map/ppermute | solution.py:23
  278.3 18.1 %copy-start.21 = (pred[128]{0:T(512)(128)(4,1)S(1)}, pred[128]{0:T(512)(128)(4,1)}, u32[]{:S(2)}) copy-start(pred[128]{0:T(512)(128)(4,1)} %get-tuple-element.17) | copy-start | bytes 388
  278.3 18.1 %copy-start.22 = (pred[128]{0:T(512)(128)(4,1)S(1)}, pred[128]{0:T(512)(128)(4,1)}, u32[]{:S(2)}) copy-start(pred[128]{0:T(512)(128)(4,1)} %get-tuple-element.92) | copy-start | bytes 388
  278.3 18.1 %copy-start.25 = (pred[128]{0:T(512)(128)(4,1)S(1)}, pred[128]{0:T(512)(128)(4,1)}, u32[]{:S(2)}) copy-start(pred[128]{0:T(512)(128)(4,1)} %get-tuple-element.75) | copy-start | bytes 388
  278.3 18.1 %copy-start.26 = (pred[128]{0:T(512)(128)(4,1)S(1)}, pred[128]{0:T(512)(128)(4,1)}, u32[]{:S(2)}) copy-start(pred[128]{0:T(512)(128)(4,1)} %get-tuple-element.77) | copy-start | bytes 388
  304.5 3.3 collective-permute-start.8
  309.7 40.4 %all-to-all-start.4 = ((f32[32,5,32,128]{3,2,1,0:T(8,128)}), f32[32,5,32,128]{3,2,1,0:T(8,128)}, u32[]{:S(2)}, u32[]{:S(2)}) async-start(f32[32,5,32,128]{3,2,1,0:T(8,128)} %stack.16), calls=%async_computation.4 | async-start | bytes 5242880 | tf_op jit(solution)/shard_map/all_to_all | solution.py:76
  318.2 7.2 %collective-permute-start.9 = (f32[5,32,128]{2,1,0:T(8,128)S(1)}, f32[5,32,128]{2,1,0:T(8,128)}, u32[]{:S(2)}, u32[]{:S(2)}) collective-permute-start(f32[5,32,128]{2,1,0:T(8,128)S(1)} %get-tuple-element.38), channel_id=1, source_target_pairs={{0,32},{32,64},{64,96},{1,33},{33,65},{65,97},{2,34},{34,66},{66,9... | collective-permute-start | bytes 245768 | tf_op jit(solution)/shard_map/ppermute | solution.py:13
  352.7 77.3 %all-to-all-start.5 = ((f32[32,5,32,128]{3,2,1,0:T(8,128)}), f32[32,5,32,128]{3,2,1,0:T(8,128)}, u32[]{:S(2)}, u32[]{:S(2)}) async-start(f32[32,5,32,128]{3,2,1,0:T(8,128)} %stack.17), calls=%async_computation.5 | async-start | bytes 5242880 | tf_op jit(solution)/shard_map/all_to_all | solution.py:76
  363.7 18.3 %collective-permute-start.10 = (f32[5,16,32,1]{2,1,3,0:T(8,128)S(1)}, f32[5,16,32,1]{2,1,3,0:T(8,128)}, u32[]{:S(2)}, u32[]{:S(2)}) collective-permute-start(f32[5,16,32,1]{2,1,3,0:T(8,128)S(1)} %copy.343), channel_id=1, source_target_pairs={{1,0},{2,1},{3,2},{4,3},{5,4},{6,5},{7,6},{8,7},{9,8},{10,9},{11,1... | collective-permute-start | bytes 30728 | tf_op jit(solution)/shard_map/ppermute | solution.py:25
  372.3 22.3 %collective-permute-start.11 = (f32[5,16,32,1]{2,1,3,0:T(8,128)}, f32[5,16,32,1]{2,1,3,0:T(8,128)}, u32[]{:S(2)}, u32[]{:S(2)}) collective-permute-start(f32[5,16,32,1]{2,1,3,0:T(8,128)} %copy.345), channel_id=1, source_target_pairs={{0,1},{1,2},{2,3},{3,4},{4,5},{5,6},{6,7},{7,8},{8,9},{9,10},{10,1... | collective-permute-start | bytes 30728 | tf_op jit(solution)/shard_map/ppermute | solution.py:23
  444.6 18.1 %copy-start.19 = (pred[128]{0:T(512)(128)(4,1)S(1)}, pred[128]{0:T(512)(128)(4,1)}, u32[]{:S(2)}) copy-start(pred[128]{0:T(512)(128)(4,1)} %get-tuple-element.9) | copy-start | bytes 388
  444.6 18.1 %copy-start.20 = (pred[128]{0:T(512)(128)(4,1)S(1)}, pred[128]{0:T(512)(128)(4,1)}, u32[]{:S(2)}) copy-start(pred[128]{0:T(512)(128)(4,1)} %get-tuple-element.90) | copy-start | bytes 388
  444.6 18.1 %copy-start.23 = (pred[128]{0:T(512)(128)(4,1)S(1)}, pred[128]{0:T(512)(128)(4,1)}, u32[]{:S(2)}) copy-start(pred[128]{0:T(512)(128)(4,1)} %get-tuple-element.6) | copy-start | bytes 388
  444.6 18.1 %copy-start.24 = (pred[128]{0:T(512)(128)(4,1)S(1)}, pred[128]{0:T(512)(128)(4,1)}, u32[]{:S(2)}) copy-start(pred[128]{0:T(512)(128)(4,1)} %get-tuple-element.73) | copy-start | bytes 388
  (17 other events, 105.1 us)
